TPU v7x, 32 devices: a whole 2x2x4 slice. The times are simulated.
32 devices in a mesh: parts: 2 (over y), cols: 4 (over z), rows: 2 (over x), rep: 2 (over core).
Axes of the slice: x: 2, y: 2, z: 4, core: 2. Of those that a mesh axis runs over, the one named last changes fastest.
Arguments:
- sources: float32 [4096, 64], P(('parts', 'rows')), parts along dimension 0, may hold values from -11 to 11
- source_mass: float32 [4096], P(('parts', 'rows')), parts along dimension 0, may hold values from 0.2 to 5
- targets: float32 [4096, 64], P(('parts', 'cols', 'rep')), parts along dimension 0, may hold values from -6 to 6
- target_mass: float32 [4096], P(('parts', 'cols', 'rep')), parts along dimension 0, may hold values from 0.2 to 5
- fate_panel: float32 [4096, 64], P(('parts', 'cols', 'rep')), parts along dimension 0, may hold values from 0 to 1
Outputs:
- f_pot: float32 [4096], P(('parts', 'rows')), parts along dimension 0
- g_pot: float32 [4096], P(('parts', 'cols', 'rep')), parts along dimension 0
- fate_rows: float32 [4096, 64], P(('parts', 'rows', 'cols', 'rep')), parts along dimension 0
There are 2 independent parts, one for each index of `parts`. A program takes and returns all parts, laid end to end along the dimension named above; each array names one. Nothing has to cross between parts.
All inputs are finite; a program needn't handle non-finite values.
Results may differ from a plain program's by a relative error of at most 0.0003.
Values sent between devices are 32-bit elements; how exact they have to be, the bound alone decides.
No kernel may reach another device: no remote copies, remote signals or barrier semaphores. Data moves between devices by JAX's collectives and lax.ppermute only.
A program may use at most 64 MiB of HBM per device.

v0:
```python
import math
import jax
import jax.numpy as jnp
from jax import lax
from jax.sharding import PartitionSpec as P

ITERS = 8
entropic = 0.1
relaxed = 1.0 / 1.1


def pair_cost(lhs_rows, lhs_sq, rhs_rows, rhs_sq):
    products = lax.dot_general(
        lhs_rows,
        rhs_rows,
        (((1,), (1,)), ((), ())),
        precision=lax.Precision.HIGHEST,
        preferred_element_type=jnp.float32,
    )
    return (lhs_sq[:, None] + rhs_sq[None, :] - 2.0 * products) / lhs_rows.shape[1]


def row_potential(maxima, totals):
    whole_peak = lax.pmax(maxima, ("cols", "rep"))
    whole_total = lax.psum(totals * jnp.exp(maxima - whole_peak), ("cols", "rep"))
    return -relaxed * entropic * (whole_peak + jnp.log(whole_total))


def col_potential(maxima, totals):
    whole_peak = lax.pmax(maxima, "rows")
    whole_total = lax.psum(totals * jnp.exp(maxima - whole_peak), "rows")
    return -relaxed * entropic * (whole_peak + jnp.log(whole_total))


def body(sources, source_mass, targets, target_mass, fate_panel):
    src_count = sources.shape[0]
    tgt_count = targets.shape[0]
    feature_dim = sources.shape[1]
    all_sources = src_count * lax.axis_size("rows")
    all_targets = tgt_count * lax.axis_size(("cols", "rep"))
    log_a = jnp.log(source_mass / all_sources)
    log_b = jnp.log(target_mass / all_targets)
    src_sq = jnp.sum(sources * sources, axis=1)
    tgt_sq = jnp.sum(targets * targets, axis=1)
    row_size = math.gcd(src_count, 512)
    block_count = src_count // row_size
    src_blocks = sources.reshape(block_count, row_size, feature_dim)
    sq_blocks = src_sq.reshape(block_count, row_size)
    loga_blocks = log_a.reshape(block_count, row_size)

    def row_scores(packed, g_pot):
        return (
            log_b[None, :]
            + (g_pot[None, :] - pair_cost(packed[0], packed[1], targets, tgt_sq)) / entropic
        )

    g_pot = jnp.zeros((tgt_count,), jnp.float32)
    f_pot = jnp.zeros((src_count,), jnp.float32)
    for iteration in range(ITERS):

        def row_per_block(packed):
            scores = row_scores(packed, g_pot)
            maxima = jnp.max(scores, axis=1)
            return (maxima, jnp.sum(jnp.exp(scores - maxima[:, None]), axis=1))

        maxima, row_totals = lax.map(row_per_block, (src_blocks, sq_blocks))
        maxima, totals = (maxima.reshape(src_count), row_totals.reshape(src_count))
        f_pot = row_potential(maxima, totals)
        f_blocks = f_pot.reshape(block_count, row_size)

        def col_per_block(running, packed):
            scores = (
                packed[2][:, None]
                + (packed[3][:, None] - pair_cost(packed[0], packed[1], targets, tgt_sq)) / entropic
            )
            highest = jnp.maximum(running[0], jnp.max(scores, axis=0))
            totals = running[1] * jnp.exp(running[0] - highest) + jnp.sum(
                jnp.exp(scores - highest[None, :]), axis=0
            )
            return ((highest, totals), None)

        initial = (
            jnp.full((tgt_count,), -jnp.inf, jnp.float32),
            jnp.zeros((tgt_count,), jnp.float32),
        )
        running, unused = lax.scan(
            col_per_block, initial, (src_blocks, sq_blocks, loga_blocks, f_blocks)
        )
        maxima, totals = running
        g_pot = col_potential(maxima, totals)

    def fate_block(packed):
        scores = row_scores(packed, g_pot)
        maxima = jnp.max(scores, axis=1)
        weights = jnp.exp(scores - maxima[:, None])
        totals = jnp.sum(weights, axis=1)
        weighted = jnp.dot(
            weights, fate_panel, precision=lax.Precision.HIGHEST, preferred_element_type=jnp.float32
        )
        return (maxima, totals, weighted)

    maxima, totals, weighted = lax.map(fate_block, (src_blocks, sq_blocks))
    maxima = maxima.reshape(src_count)
    totals = totals.reshape(src_count)
    weighted = weighted.reshape(src_count, fate_panel.shape[1])
    whole_peak = lax.pmax(maxima, ("cols", "rep"))
    factor = jnp.exp(maxima - whole_peak)
    part_weighted, part_total = (
        lax.psum_scatter(
            weighted * factor[:, None], ("cols", "rep"), scatter_dimension=0, tiled=True
        ),
        lax.psum_scatter(totals * factor, ("cols", "rep"), scatter_dimension=0, tiled=True),
    )
    fate_rows = part_weighted / part_total[:, None]
    return (f_pot, g_pot, fate_rows)


def solution(mesh):
    in_specs = (
        P(("parts", "rows"), None),
        P(("parts", "rows")),
        P(("parts", "cols", "rep"), None),
        P(("parts", "cols", "rep")),
        P(("parts", "cols", "rep"), None),
    )
    out_specs = (
        P(("parts", "rows")),
        P(("parts", "cols", "rep")),
        P(("parts", "rows", "cols", "rep"), None),
    )
    return jax.shard_map(body, mesh=mesh, in_specs=in_specs, out_specs=out_specs, check_vma=False)
```

profile of v0, /device:TPU:0, one launch (start us, length us, event | category | flops | bytes accessed | tf_op | source)
XLA Modules:
  0.0 399.3 jit_solution(12835680924114328844)
XLA Ops:
  11.3 18.1 %pmax.119 = f32[1024]{0:T(1024)S(1)} all-reduce(f32[1024]{0:T(1024)S(1)} %bitcast.428), channel_id=1, replica_groups=mesh['parts'=2,'cols'=4,'rows'=2,'rep'=2] {'cols','rep'}, use_global_device_ids=true, to_apply=%region_6.7 | all-reduce | flops 1024 | bytes 8192 | tf_op jit(solution)/shard_map/pmax | solution.py:24
  29.5 13.6 %psum.112 = f32[1024]{0:T(1024)S(1)} all-reduce(f32[1024]{0:T(1024)S(1)} %exponential_multiply_fusion.7), channel_id=1, replica_groups=mesh['parts'=2,'cols'=4,'rows'=2,'rep'=2] {'cols','rep'}, use_global_device_ids=true, to_apply=%region_7.8 | all-reduce | flops 1024 | bytes 8192 | tf_op jit(solution)/shard_map/psum | solution.py:25
  44.8 4.9 %pmax.120 = f32[256]{0:T(256)S(1)} all-reduce(f32[256]{0:T(256)S(1)} %get-tuple-element.827), channel_id=1, replica_groups=mesh['parts'=2,'cols'=4,'rows'=2,'rep'=2] {'rows'}, use_global_device_ids=true, to_apply=%region_12.13 | all-reduce | flops 256 | bytes 2048 | tf_op jit(solution)/shard_map/pmax | solution.py:30
  56.6 13.6 %pmax.121 = f32[1024]{0:T(1024)S(1)} all-reduce(f32[1024]{0:T(1024)S(1)} %bitcast.430), channel_id=1, replica_groups=mesh['parts'=2,'cols'=4,'rows'=2,'rep'=2] {'cols','rep'}, use_global_device_ids=true, to_apply=%region_18.19 | all-reduce | flops 1024 | bytes 8192 | tf_op jit(solution)/shard_map/pmax | solution.py:24
  70.2 13.6 %psum.114 = f32[1024]{0:T(1024)S(1)} all-reduce(f32[1024]{0:T(1024)S(1)} %exponential_multiply_fusion.6), channel_id=1, replica_groups=mesh['parts'=2,'cols'=4,'rows'=2,'rep'=2] {'cols','rep'}, use_global_device_ids=true, to_apply=%region_19.20 | all-reduce | flops 1024 | bytes 8192 | tf_op jit(solution)/shard_map/psum | solution.py:25
  85.6 4.9 %pmax.122 = f32[256]{0:T(256)S(1)} all-reduce(f32[256]{0:T(256)S(1)} %get-tuple-element.831), channel_id=1, replica_groups=mesh['parts'=2,'cols'=4,'rows'=2,'rep'=2] {'rows'}, use_global_device_ids=true, to_apply=%region_24.25 | all-reduce | flops 256 | bytes 2048 | tf_op jit(solution)/shard_map/pmax | solution.py:30
  97.4 13.6 %pmax.123 = f32[1024]{0:T(1024)S(1)} all-reduce(f32[1024]{0:T(1024)S(1)} %bitcast.432), channel_id=1, replica_groups=mesh['parts'=2,'cols'=4,'rows'=2,'rep'=2] {'cols','rep'}, use_global_device_ids=true, to_apply=%region_30.31 | all-reduce | flops 1024 | bytes 8192 | tf_op jit(solution)/shard_map/pmax | solution.py:24
  111.0 13.6 %psum.116 = f32[1024]{0:T(1024)S(1)} all-reduce(f32[1024]{0:T(1024)S(1)} %exponential_multiply_fusion.5), channel_id=1, replica_groups=mesh['parts'=2,'cols'=4,'rows'=2,'rep'=2] {'cols','rep'}, use_global_device_ids=true, to_apply=%region_31.32 | all-reduce | flops 1024 | bytes 8192 | tf_op jit(solution)/shard_map/psum | solution.py:25
  126.4 4.9 %pmax.124 = f32[256]{0:T(256)S(1)} all-reduce(f32[256]{0:T(256)S(1)} %get-tuple-element.835), channel_id=1, replica_groups=mesh['parts'=2,'cols'=4,'rows'=2,'rep'=2] {'rows'}, use_global_device_ids=true, to_apply=%region_36.37 | all-reduce | flops 256 | bytes 2048 | tf_op jit(solution)/shard_map/pmax | solution.py:30
  138.2 13.6 %pmax.125 = f32[1024]{0:T(1024)S(1)} all-reduce(f32[1024]{0:T(1024)S(1)} %bitcast.434), channel_id=1, replica_groups=mesh['parts'=2,'cols'=4,'rows'=2,'rep'=2] {'cols','rep'}, use_global_device_ids=true, to_apply=%region_42.43 | all-reduce | flops 1024 | bytes 8192 | tf_op jit(solution)/shard_map/pmax | solution.py:24
  151.8 13.6 %psum.118 = f32[1024]{0:T(1024)S(1)} all-reduce(f32[1024]{0:T(1024)S(1)} %exponential_multiply_fusion.4), channel_id=1, replica_groups=mesh['parts'=2,'cols'=4,'rows'=2,'rep'=2] {'cols','rep'}, use_global_device_ids=true, to_apply=%region_43.44 | all-reduce | flops 1024 | bytes 8192 | tf_op jit(solution)/shard_map/psum | solution.py:25
  179.0 13.6 %pmax.127 = f32[1024]{0:T(1024)S(1)} all-reduce(f32[1024]{0:T(1024)S(1)} %bitcast.436), channel_id=1, replica_groups=mesh['parts'=2,'cols'=4,'rows'=2,'rep'=2] {'cols','rep'}, use_global_device_ids=true, to_apply=%region_54.55 | all-reduce | flops 1024 | bytes 8192 | tf_op jit(solution)/shard_map/pmax | solution.py:24
  192.6 13.6 %psum.120 = f32[1024]{0:T(1024)S(1)} all-reduce(f32[1024]{0:T(1024)S(1)} %exponential_multiply_fusion.3), channel_id=1, replica_groups=mesh['parts'=2,'cols'=4,'rows'=2,'rep'=2] {'cols','rep'}, use_global_device_ids=true, to_apply=%region_55.56 | all-reduce | flops 1024 | bytes 8192 | tf_op jit(solution)/shard_map/psum | solution.py:25
  212.9 5.1 %psum.121 = f32[256]{0:T(256)S(1)} all-reduce(f32[256]{0:T(256)S(1)} %exponential_multiply_fusion.11), channel_id=1, replica_groups=mesh['parts'=2,'cols'=4,'rows'=2,'rep'=2] {'rows'}, use_global_device_ids=true, to_apply=%region_61.62 | all-reduce | flops 256 | bytes 2048 | tf_op jit(solution)/shard_map/psum | solution.py:31
  220.0 13.6 %pmax.129 = f32[1024]{0:T(1024)S(1)} all-reduce(f32[1024]{0:T(1024)S(1)} %bitcast.438), channel_id=1, replica_groups=mesh['parts'=2,'cols'=4,'rows'=2,'rep'=2] {'cols','rep'}, use_global_device_ids=true, to_apply=%region_66.67 | all-reduce | flops 1024 | bytes 8192 | tf_op jit(solution)/shard_map/pmax | solution.py:24
  233.6 13.6 %psum.122 = f32[1024]{0:T(1024)S(1)} all-reduce(f32[1024]{0:T(1024)S(1)} %exponential_multiply_fusion.2), channel_id=1, replica_groups=mesh['parts'=2,'cols'=4,'rows'=2,'rep'=2] {'cols','rep'}, use_global_device_ids=true, to_apply=%region_67.68 | all-reduce | flops 1024 | bytes 8192 | tf_op jit(solution)/shard_map/psum | solution.py:25
  260.8 13.6 %pmax.131 = f32[1024]{0:T(1024)S(1)} all-reduce(f32[1024]{0:T(1024)S(1)} %bitcast.440), channel_id=1, replica_groups=mesh['parts'=2,'cols'=4,'rows'=2,'rep'=2] {'cols','rep'}, use_global_device_ids=true, to_apply=%region_78.79 | all-reduce | flops 1024 | bytes 8192 | tf_op jit(solution)/shard_map/pmax | solution.py:24
  274.4 13.6 %psum.124 = f32[1024]{0:T(1024)S(1)} all-reduce(f32[1024]{0:T(1024)S(1)} %exponential_multiply_fusion.1), channel_id=1, replica_groups=mesh['parts'=2,'cols'=4,'rows'=2,'rep'=2] {'cols','rep'}, use_global_device_ids=true, to_apply=%region_79.80 | all-reduce | flops 1024 | bytes 8192 | tf_op jit(solution)/shard_map/psum | solution.py:25
  301.6 13.6 %pmax.133 = f32[1024]{0:T(1024)S(1)} all-reduce(f32[1024]{0:T(1024)S(1)} %bitcast.442), channel_id=1, replica_groups=mesh['parts'=2,'cols'=4,'rows'=2,'rep'=2] {'cols','rep'}, use_global_device_ids=true, to_apply=%region_90.91 | all-reduce | flops 1024 | bytes 8192 | tf_op jit(solution)/shard_map/pmax | solution.py:24
  315.2 13.6 %psum.126 = f32[1024]{0:T(1024)S(1)} all-reduce(f32[1024]{0:T(1024)S(1)} %exponential_multiply_fusion), channel_id=1, replica_groups=mesh['parts'=2,'cols'=4,'rows'=2,'rep'=2] {'cols','rep'}, use_global_device_ids=true, to_apply=%region_91.92 | all-reduce | flops 1024 | bytes 8192 | tf_op jit(solution)/shard_map/psum | solution.py:25
  341.0 5.7 %while.222 = (s32[]{:T(128)}, f32[2,512]{1,0:T(2,128)S(1)}, f32[2,512]{1,0:T(2,128)S(1)}, f32[2,512,64]{1,0,2:T(2,128)S(1)}, f32[256]{0:T(256)S(1)}, /*index=5*/...) while((s32[]{:T(128)}, f32[2,512]{1,0:T(2,128)S(1)}, ...), condition=%wide.region_101.102_spmd, body=%wide.region_98.101_spmd.sunk | while | flops 202767360 | bytes 2647193 | solution.py:102
  347.3 13.6 %pmax.135 = f32[1024]{0:T(1024)S(1)} all-reduce(f32[1024]{0:T(1024)S(1)} %bitcast.426), channel_id=1, replica_groups=mesh['parts'=2,'cols'=4,'rows'=2,'rep'=2] {'cols','rep'}, use_global_device_ids=true, to_apply=%region_102.103 | all-reduce | flops 1024 | bytes 8192 | tf_op jit(solution)/shard_map/pmax | solution.py:106
  363.6 13.7 %all-reduce = f32[1024]{0:T(1024)S(1)} all-reduce(f32[1024]{0:T(1024)S(1)} %get-tuple-element.1408), channel_id=3, replica_groups=mesh['parts'=2,'cols'=4,'rows'=2,'rep'=2] {'cols','rep'}, use_global_device_ids=true, to_apply=%region_104.105.clone | all-reduce | flops 1024 | bytes 8192
  377.3 13.7 %reduce-scatter.2.cloned.1.call-done = f32[128,64]{0,1:T(8,128)} async-done(((f32[1024,64]{0,1:T(8,128)}), f32[128,64]{0,1:T(8,128)}) %reduce-scatter.2.cloned.1.call-update) | async-done | bytes 32784 | tf_op jit(solution)/shard_map/reduce_scatter | solution.py:109
  (360 shorter events, 129.0 us)
Async XLA Ops:
  7.2 1.2 copy-start.1
  7.2 383.9 %reduce-scatter.2.cloned.1.call-start = ((), (), s32[]{:S(2)}) async-start(), calls=%async_computation.1 | async-start | bytes 294912 | tf_op jit(solution)/shard_map/reduce_scatter | solution.py:109
  8.4 1.0 copy-start.2
  8.6 0.7 copy-start.4
  8.6 0.7 copy-start.6
  328.8 0.6 copy-start.3
  329.4 11.6 %copy-start = (f32[256,64]{0,1:T(8,128)S(1)}, f32[256,64]{0,1:T(8,128)}, u32[]{:S(2)}) copy-start(f32[256,64]{0,1:T(8,128)} %param.43) | copy-start | bytes 196612
  346.7 0.6 copy-start.5
  361.7 0.7 copy-start.7
Sparse Core Ops, SparseCore 0:
  361.8 29.2 reduce-scatter.1
where the time goes:
time: 400 us; the launch traced here: 399 us
  blocking collectives  328 us (82%)
  matrix products  24.7 us (6%)
  between operations  15.2 us (4%)
  waiting for transfers between devices  13.8 us (3%)
  local copies, waits for them, and re-layouts  8.2 us (2%)
  other arithmetic  7.79 us (2%)
    pmax x8, blocking collectives, row_potential(): whole_peak = lax.pmax(maxima, ('cols', 'rep'))  113 us
    psum x8, blocking collectives, row_potential(): lax.psum(totals * jnp.exp(maxima - whole_peak), ('cols', 'rep'))  109 us
    psum x8, blocking collectives, col_potential(): whole_total = lax.psum(totals * jnp.exp(maxima - whole_peak), 'rows')  39.5 us
    pmax x8, blocking collectives, col_potential(): whole_peak = lax.pmax(maxima, 'rows')  39.5 us
    dot_general x34, matrix products, pair_cost(): lax.dot_general(lhs_rows, rhs_rows, (((1,), (1,)), ((), ())), precision=l...  23.7 us
    reduce_scatter x1, waiting for transfers between devices, body(): lax.psum_scatter(weighted * factor[:, None], ('cols', 'rep'), scatter_dim...  13.7 us
    unnamed x1, blocking collectives  13.7 us
    pmax x1, blocking collectives, body(): whole_peak = lax.pmax(maxima, ('cols', 'rep'))  13.6 us
  transfers between devices with their start and end apart: 1, of which 1 were waited for; matrix products, arithmetic and copies ran while one was open for 0% of the time, Pallas kernels for 0%

commit v1 on v0

--- a/solution.py
+++ b/solution.py
@@ -28,7 +28,7 @@
 
 def col_potential(maxima, totals):
     whole_peak = lax.pmax(maxima, "rows")
-    whole_total = lax.psum(totals * jnp.exp(maxima - whole_peak), "rows")
+    whole_total = jnp.sum(lax.all_gather(totals * jnp.exp(maxima - whole_peak), "rows"), axis=0)
     return -relaxed * entropic * (whole_peak + jnp.log(whole_total))
 
 

time: 400 us -> 395 us (0.988)
  blocking collectives: 328 us -> 323 us
    psum x8 -> x0, blocking collectives: 39.5 us -> none  [col_potential(): whole_total = lax.psum(totals * jnp.exp(maxima - whole_peak), 'rows')]
    all_gather x0 -> x8, blocking collectives: none -> 34.1 us  [col_potential(): lax.all_gather(totals * jnp.exp(maxima - whole_peak), 'rows')]
where the time goes in v1:
time: 395 us; the launch traced here: 394 us
  blocking collectives  323 us (82%)
  matrix products  24.7 us (6%)
  between operations  15.3 us (4%)
  waiting for transfers between devices  13.6 us (3%)
  local copies, waits for them, and re-layouts  8.21 us (2%)
  other arithmetic  7.95 us (2%)
    pmax x8, blocking collectives, row_potential(): whole_peak = lax.pmax(maxima, ('cols', 'rep'))  113 us
    psum x8, blocking collectives, row_potential(): lax.psum(totals * jnp.exp(maxima - whole_peak), ('cols', 'rep'))  109 us
    pmax x8, blocking collectives, col_potential(): whole_peak = lax.pmax(maxima, 'rows')  39.5 us
    all_gather x8, blocking collectives, col_potential(): lax.all_gather(totals * jnp.exp(maxima - whole_peak), 'rows')  34.1 us
    dot_general x34, matrix products, pair_cost(): lax.dot_general(lhs_rows, rhs_rows, (((1,), (1,)), ((), ())), precision=l...  23.7 us
    unnamed x1, blocking collectives  13.7 us
    pmax x1, blocking collectives, body(): whole_peak = lax.pmax(maxima, ('cols', 'rep'))  13.6 us
    reduce_scatter x1, waiting for transfers between devices, body(): lax.psum_scatter(weighted * factor[:, None], ('cols', 'rep'), scatter_dim...  13.6 us
  transfers between devices with their start and end apart: 1, of which 1 were waited for; matrix products, arithmetic and copies ran while one was open for 0% of the time, Pallas kernels for 0%

profile of v1, /device:TPU:0, one launch (start us, length us, event | category | flops | bytes accessed | tf_op | source)
XLA Modules:
  0.0 393.9 jit_solution(7241451888707832330)
XLA Ops:
  11.3 18.1 %pmax.119 = f32[1024]{0:T(1024)S(1)} all-reduce(f32[1024]{0:T(1024)S(1)} %bitcast.436), channel_id=1, replica_groups=mesh['parts'=2,'cols'=4,'rows'=2,'rep'=2] {'cols','rep'}, use_global_device_ids=true, to_apply=%region_6.7 | all-reduce | flops 1024 | bytes 8192 | tf_op jit(solution)/shard_map/pmax | solution.py:24
  29.5 13.6 %psum.56 = f32[1024]{0:T(1024)S(1)} all-reduce(f32[1024]{0:T(1024)S(1)} %exponential_multiply_fusion.7), channel_id=1, replica_groups=mesh['parts'=2,'cols'=4,'rows'=2,'rep'=2] {'cols','rep'}, use_global_device_ids=true, to_apply=%region_7.8 | all-reduce | flops 1024 | bytes 8192 | tf_op jit(solution)/shard_map/psum | solution.py:25
  44.8 4.9 %pmax.120 = f32[256]{0:T(256)S(1)} all-reduce(f32[256]{0:T(256)S(1)} %get-tuple-element.827), channel_id=1, replica_groups=mesh['parts'=2,'cols'=4,'rows'=2,'rep'=2] {'rows'}, use_global_device_ids=true, to_apply=%region_12.13 | all-reduce | flops 256 | bytes 2048 | tf_op jit(solution)/shard_map/pmax | solution.py:30
  56.0 13.6 %pmax.121 = f32[1024]{0:T(1024)S(1)} all-reduce(f32[1024]{0:T(1024)S(1)} %bitcast.438), channel_id=1, replica_groups=mesh['parts'=2,'cols'=4,'rows'=2,'rep'=2] {'cols','rep'}, use_global_device_ids=true, to_apply=%region_18.19 | all-reduce | flops 1024 | bytes 8192 | tf_op jit(solution)/shard_map/pmax | solution.py:24
  69.6 13.6 %psum.57 = f32[1024]{0:T(1024)S(1)} all-reduce(f32[1024]{0:T(1024)S(1)} %exponential_multiply_fusion.6), channel_id=1, replica_groups=mesh['parts'=2,'cols'=4,'rows'=2,'rep'=2] {'cols','rep'}, use_global_device_ids=true, to_apply=%region_19.20 | all-reduce | flops 1024 | bytes 8192 | tf_op jit(solution)/shard_map/psum | solution.py:25
  84.9 4.9 %pmax.122 = f32[256]{0:T(256)S(1)} all-reduce(f32[256]{0:T(256)S(1)} %get-tuple-element.831), channel_id=1, replica_groups=mesh['parts'=2,'cols'=4,'rows'=2,'rep'=2] {'rows'}, use_global_device_ids=true, to_apply=%region_24.25 | all-reduce | flops 256 | bytes 2048 | tf_op jit(solution)/shard_map/pmax | solution.py:30
  96.1 13.6 %pmax.123 = f32[1024]{0:T(1024)S(1)} all-reduce(f32[1024]{0:T(1024)S(1)} %bitcast.440), channel_id=1, replica_groups=mesh['parts'=2,'cols'=4,'rows'=2,'rep'=2] {'cols','rep'}, use_global_device_ids=true, to_apply=%region_30.31 | all-reduce | flops 1024 | bytes 8192 | tf_op jit(solution)/shard_map/pmax | solution.py:24
  109.7 13.6 %psum.58 = f32[1024]{0:T(1024)S(1)} all-reduce(f32[1024]{0:T(1024)S(1)} %exponential_multiply_fusion.5), channel_id=1, replica_groups=mesh['parts'=2,'cols'=4,'rows'=2,'rep'=2] {'cols','rep'}, use_global_device_ids=true, to_apply=%region_31.32 | all-reduce | flops 1024 | bytes 8192 | tf_op jit(solution)/shard_map/psum | solution.py:25
  125.1 4.9 %pmax.124 = f32[256]{0:T(256)S(1)} all-reduce(f32[256]{0:T(256)S(1)} %get-tuple-element.835), channel_id=1, replica_groups=mesh['parts'=2,'cols'=4,'rows'=2,'rep'=2] {'rows'}, use_global_device_ids=true, to_apply=%region_36.37 | all-reduce | flops 256 | bytes 2048 | tf_op jit(solution)/shard_map/pmax | solution.py:30
  136.2 13.6 %pmax.125 = f32[1024]{0:T(1024)S(1)} all-reduce(f32[1024]{0:T(1024)S(1)} %bitcast.442), channel_id=1, replica_groups=mesh['parts'=2,'cols'=4,'rows'=2,'rep'=2] {'cols','rep'}, use_global_device_ids=true, to_apply=%region_42.43 | all-reduce | flops 1024 | bytes 8192 | tf_op jit(solution)/shard_map/pmax | solution.py:24
  149.9 13.6 %psum.59 = f32[1024]{0:T(1024)S(1)} all-reduce(f32[1024]{0:T(1024)S(1)} %exponential_multiply_fusion.4), channel_id=1, replica_groups=mesh['parts'=2,'cols'=4,'rows'=2,'rep'=2] {'cols','rep'}, use_global_device_ids=true, to_apply=%region_43.44 | all-reduce | flops 1024 | bytes 8192 | tf_op jit(solution)/shard_map/psum | solution.py:25
  176.4 13.6 %pmax.127 = f32[1024]{0:T(1024)S(1)} all-reduce(f32[1024]{0:T(1024)S(1)} %bitcast.444), channel_id=1, replica_groups=mesh['parts'=2,'cols'=4,'rows'=2,'rep'=2] {'cols','rep'}, use_global_device_ids=true, to_apply=%region_54.55 | all-reduce | flops 1024 | bytes 8192 | tf_op jit(solution)/shard_map/pmax | solution.py:24
  190.0 13.6 %psum.60 = f32[1024]{0:T(1024)S(1)} all-reduce(f32[1024]{0:T(1024)S(1)} %exponential_multiply_fusion.3), channel_id=1, replica_groups=mesh['parts'=2,'cols'=4,'rows'=2,'rep'=2] {'cols','rep'}, use_global_device_ids=true, to_apply=%region_55.56 | all-reduce | flops 1024 | bytes 8192 | tf_op jit(solution)/shard_map/psum | solution.py:25
  216.7 13.6 %pmax.129 = f32[1024]{0:T(1024)S(1)} all-reduce(f32[1024]{0:T(1024)S(1)} %bitcast.446), channel_id=1, replica_groups=mesh['parts'=2,'cols'=4,'rows'=2,'rep'=2] {'cols','rep'}, use_global_device_ids=true, to_apply=%region_66.67 | all-reduce | flops 1024 | bytes 8192 | tf_op jit(solution)/shard_map/pmax | solution.py:24
  230.3 13.6 %psum.61 = f32[1024]{0:T(1024)S(1)} all-reduce(f32[1024]{0:T(1024)S(1)} %exponential_multiply_fusion.2), channel_id=1, replica_groups=mesh['parts'=2,'cols'=4,'rows'=2,'rep'=2] {'cols','rep'}, use_global_device_ids=true, to_apply=%region_67.68 | all-reduce | flops 1024 | bytes 8192 | tf_op jit(solution)/shard_map/psum | solution.py:25
  256.9 13.6 %pmax.131 = f32[1024]{0:T(1024)S(1)} all-reduce(f32[1024]{0:T(1024)S(1)} %bitcast.448), channel_id=1, replica_groups=mesh['parts'=2,'cols'=4,'rows'=2,'rep'=2] {'cols','rep'}, use_global_device_ids=true, to_apply=%region_78.79 | all-reduce | flops 1024 | bytes 8192 | tf_op jit(solution)/shard_map/pmax | solution.py:24
  270.5 13.6 %psum.62 = f32[1024]{0:T(1024)S(1)} all-reduce(f32[1024]{0:T(1024)S(1)} %exponential_multiply_fusion.1), channel_id=1, replica_groups=mesh['parts'=2,'cols'=4,'rows'=2,'rep'=2] {'cols','rep'}, use_global_device_ids=true, to_apply=%region_79.80 | all-reduce | flops 1024 | bytes 8192 | tf_op jit(solution)/shard_map/psum | solution.py:25
  285.8 4.9 %pmax.132 = f32[256]{0:T(256)S(1)} all-reduce(f32[256]{0:T(256)S(1)} %get-tuple-element.851), channel_id=1, replica_groups=mesh['parts'=2,'cols'=4,'rows'=2,'rep'=2] {'rows'}, use_global_device_ids=true, to_apply=%region_84.85 | all-reduce | flops 256 | bytes 2048 | tf_op jit(solution)/shard_map/pmax | solution.py:30
  297.0 13.6 %pmax.133 = f32[1024]{0:T(1024)S(1)} all-reduce(f32[1024]{0:T(1024)S(1)} %bitcast.450), channel_id=1, replica_groups=mesh['parts'=2,'cols'=4,'rows'=2,'rep'=2] {'cols','rep'}, use_global_device_ids=true, to_apply=%region_90.91 | all-reduce | flops 1024 | bytes 8192 | tf_op jit(solution)/shard_map/pmax | solution.py:24
  310.6 13.6 %psum.63 = f32[1024]{0:T(1024)S(1)} all-reduce(f32[1024]{0:T(1024)S(1)} %exponential_multiply_fusion), channel_id=1, replica_groups=mesh['parts'=2,'cols'=4,'rows'=2,'rep'=2] {'cols','rep'}, use_global_device_ids=true, to_apply=%region_91.92 | all-reduce | flops 1024 | bytes 8192 | tf_op jit(solution)/shard_map/psum | solution.py:25
  335.8 5.7 %while.222 = (s32[]{:T(128)}, f32[2,512]{1,0:T(2,128)S(1)}, f32[2,512]{1,0:T(2,128)S(1)}, f32[2,512,64]{1,0,2:T(2,128)S(1)}, f32[256]{0:T(256)S(1)}, /*index=5*/...) while((s32[]{:T(128)}, f32[2,512]{1,0:T(2,128)S(1)}, ...), condition=%wide.region_101.102_spmd, body=%wide.region_98.101_spmd.sunk | while | flops 202767360 | bytes 2647193 | solution.py:102
  342.1 13.6 %pmax.135 = f32[1024]{0:T(1024)S(1)} all-reduce(f32[1024]{0:T(1024)S(1)} %bitcast.434), channel_id=1, replica_groups=mesh['parts'=2,'cols'=4,'rows'=2,'rep'=2] {'cols','rep'}, use_global_device_ids=true, to_apply=%region_102.103 | all-reduce | flops 1024 | bytes 8192 | tf_op jit(solution)/shard_map/pmax | solution.py:106
  358.4 13.7 %all-reduce = f32[1024]{0:T(1024)S(1)} all-reduce(f32[1024]{0:T(1024)S(1)} %get-tuple-element.1408), channel_id=11, replica_groups=mesh['parts'=2,'cols'=4,'rows'=2,'rep'=2] {'cols','rep'}, use_global_device_ids=true, to_apply=%region_104.105.clone | all-reduce | flops 1024 | bytes 8192
  372.1 13.6 %reduce-scatter.2.cloned.1.call-done = f32[128,64]{0,1:T(8,128)} async-done(((f32[1024,64]{0,1:T(8,128)}), f32[128,64]{0,1:T(8,128)}) %reduce-scatter.2.cloned.1.call-update) | async-done | bytes 32784 | tf_op jit(solution)/shard_map/reduce_scatter | solution.py:109
  (368 shorter events, 123.9 us)
Async XLA Ops:
  7.2 1.2 copy-start.1
  7.2 378.5 %reduce-scatter.2.cloned.1.call-start = ((), (), s32[]{:S(2)}) async-start(), calls=%async_computation.1 | async-start | bytes 294912 | tf_op jit(solution)/shard_map/reduce_scatter | solution.py:109
  8.4 1.0 copy-start.2
  8.6 0.7 copy-start.4
  8.6 0.7 copy-start.6
  324.2 0.6 copy-start.3
  324.8 10.9 %copy-start = (f32[256,64]{0,1:T(8,128)S(1)}, f32[256,64]{0,1:T(8,128)}, u32[]{:S(2)}) copy-start(f32[256,64]{0,1:T(8,128)} %param.43) | copy-start | bytes 196612
  341.5 0.6 copy-start.5
  356.5 0.7 copy-start.7
Sparse Core Ops, SparseCore 0:
  356.6 29.0 reduce-scatter.1
